TPU v7x, 32 devices: a whole 2x2x4 slice. The times are simulated.
32 devices in a mesh: pair: 8 (over z, y), virt: 4 (over x, core).
Axes of the slice: x: 2, y: 2, z: 4, core: 2. Of those that a mesh axis runs over, the one named last changes fastest.
Arguments:
- amps_pm: bfloat16 [64, 64, 4096], P(('pair', 'virt')), may hold values from -6 to 6
- integrals: bfloat16 [32, 4096, 2048], P(('pair', 'virt')), may hold values from -0.046875 to 0.046875
- fock_vv: bfloat16 [512, 512], replicated, may hold values from -0.25 to 0.25
- blk_tiles: int32 [32, 2], replicated, may hold values from 0 to 63, as said below
- blk_mask: int32 [32], replicated, may hold values 0 or 1
Outputs:
- sigma: bfloat16 [64, 64, 2048], P('pair', 'virt')
Inputs may be any that keep to these rules, and one draw needn't show every extreme that they name: Each row is (input tile pair, output tile pair). Integral tile r belongs to device r // 1 of the joined axis pair+virt, and its input tile pair lies in that device's virt slab: blk_tiles[r, 0] // 16 == (r) % 4. No two rows are equal.
All inputs are finite; a program needn't handle non-finite values.
Results may differ from a plain program's by a relative error of at most 0.0033.
Values may be sent and summed in bfloat16 or wider, within the bound.
No kernel may reach another device: no remote copies, remote signals or barrier semaphores. Data moves between devices by JAX's collectives and lax.ppermute only.
A program may use at most 128 MiB of HBM per device.

v0:
```python
import jax
import jax.numpy as jnp
from jax import lax
from jax.sharding import PartitionSpec as P

TILE = 64
NVT = 8
AS = 32


def per_device(amps_pm, integrals, fock_vv, blk_tiles, blk_mask):
    n_virt = lax.axis_size("virt")
    n_pair = lax.axis_size("pair")
    n_dev = n_virt * n_pair
    pm_rows, n_tiles, tile_len = amps_pm.shape
    out_cols = integrals.shape[2]
    slab = n_tiles // n_virt
    device = lax.axis_index(("pair", "virt"))
    virt_idx = lax.axis_index("virt")
    p_grp = pm_rows * n_virt
    tin_all = blk_tiles[:, 0]
    picked = jnp.take(amps_pm, tin_all, axis=1)
    picked = jnp.transpose(picked, (1, 0, 2))
    chosen = lax.all_to_all(picked, ("pair", "virt"), 0, 0, tiled=True)
    chosen = chosen.reshape(n_dev * pm_rows, tile_len)
    sub = lax.all_to_all(amps_pm[:, :, :out_cols], "virt", split_axis=1, concat_axis=0, tiled=True)
    sub = sub.reshape(p_grp, slab // NVT, NVT, AS, TILE)
    fock_four = fock_vv.reshape(NVT, TILE, NVT, TILE)
    onebody = jnp.einsum(
        "pkqsd,bjqd->pkbsj", sub, fock_four, preferred_element_type=jnp.float32
    ).reshape(p_grp, slab, out_cols)
    own_tiles = lax.dynamic_index_in_dim(blk_tiles, device, 0, keepdims=False)
    own_mask = lax.dynamic_index_in_dim(blk_mask, device, 0, keepdims=False)
    product = jnp.dot(chosen, integrals[0], preferred_element_type=jnp.float32)
    product = (product * own_mask.astype(jnp.float32)).astype(jnp.bfloat16)
    dest_virt = own_tiles[1] // slab
    select = (jnp.arange(n_virt, dtype=jnp.int32) == dest_virt).astype(jnp.bfloat16)
    outgoing = product.reshape(n_pair, 1, p_grp, out_cols) * select[None, :, None, None]
    outgoing = outgoing.reshape(n_dev, p_grp, out_cols)
    received = lax.all_to_all(outgoing, ("pair", "virt"), 0, 0, tiled=True)
    my_tiles = virt_idx * slab + jnp.arange(slab, dtype=jnp.int32)
    one_hot = (blk_tiles[:, 1][:, None] == my_tiles[None, :]).astype(jnp.bfloat16)
    ladder = jnp.einsum("rpo,rt->pto", received, one_hot, preferred_element_type=jnp.float32)
    return (ladder + onebody).astype(jnp.bfloat16)


def solution(mesh):
    return jax.shard_map(
        per_device,
        mesh=mesh,
        in_specs=(P(("pair", "virt"), None, None), P(("pair", "virt"), None, None), P(), P(), P()),
        out_specs=P("pair", "virt", None),
        check_vma=False,
    )
```

profile of v0, /device:TPU:0, one launch (start us, length us, event | category | flops | bytes accessed | tf_op | source)
XLA Modules:
  0.0 75.2 jit_solution(7322697430825926333)
XLA Ops:
  0.0 0.8 %slice_bitcast_fusion = (s32[32]{0:T(128)S(1)}, s32[32]{0:T(128)S(1)}) fusion(s32[32,2]{0,1:T(2,128)} %param.8), kind=kLoop, calls=%fused_computation.24 | loop fusion | flops 96 | bytes 512 | tf_op jit(solution)/shard_map/eq | solution.py:42
  0.8 0.7 and_bitcast_fusion
  1.5 2.6 %gather_fusion = bf16[32,2,4096]{2,0,1:T(8,128)(2,1)S(1)} fusion(bf16[2,64,4096]{2,1,0:T(8,128)(2,1)} %param.5, s32[1024]{0:T(1024)S(1)} %pad_clamp_fusion), kind=kCustom, calls=%fused_computation | custom fusion | bytes 1048704 | tf_op jit(solution)/shard_map/jit(_take)/gather | solution.py:22
  4.0 0.1 broadcast_select_fusion
  4.2 1.3 %copy.15 = bf16[32,2,4096]{2,1,0:T(2,128)(2,1)} copy(bf16[32,2,4096]{2,0,1:T(8,128)(2,1)S(1)} %broadcast_select_fusion) | data formatting | bytes 1048576 | tf_op jit(solution)/shard_map/jit(_take)/select_n | solution.py:22
  5.5 0.0 copy-start
  5.5 7.3 %all-to-all-start = ((bf16[32,2,4096]{2,1,0:T(2,128)(2,1)}), bf16[32,2,4096]{2,1,0:T(2,128)(2,1)S(1)}, u32[]{:S(2)}, u32[]{:S(2)}) async-start(bf16[32,2,4096]{2,1,0:T(2,128)(2,1)} %copy.15), calls=%async_computation | async-start | bytes 1048576 | tf_op jit(solution)/shard_map/all_to_all | solution.py:24
  12.8 1.1 %slice.16 = bf16[2,64,2048]{2,1,0:T(8,128)(2,1)S(1)} slice(bf16[2,64,4096]{2,1,0:T(8,128)(2,1)} %param.5), slice={[0:2], [0:64], [0:2048]} | slice | bytes 1048576 | tf_op jit(solution)/shard_map/slice | solution.py:26
  13.9 0.8 %constant_dynamic-slice_fusion = s32[1,2]{0,1:T(2,128)S(1)} fusion(s32[32,2]{0,1:T(2,128)} %param.8, s32[]{:T(128)S(6)} %select_n.29), kind=kLoop, calls=%fused_computation.25 | loop fusion | bytes 20 | tf_op jit(solution)/shard_map/jit(dynamic_index_in_dim)/dynamic_slice | solution.py:32
  14.7 0.5 slice.15
  17.1 1.3 %copy.25 = bf16[2,64,2048]{2,0,1:T(2,128)(2,1)} copy(bf16[2,64,2048]{2,1,0:T(8,128)(2,1)S(1)} %slice.16) | data formatting | bytes 1048576
  19.1 0.1 mul.42
  19.2 1.3 %dynamic_slice.8 = s32[1]{0:T(128)} dynamic-slice(s32[32]{0:T(128)} %param.9, s32[]{:T(128)S(6)} %select_n.29), dynamic_slice_sizes={1} | dynamic-slice | bytes 12 | tf_op jit(solution)/shard_map/jit(dynamic_index_in_dim)/dynamic_slice | solution.py:33
  21.1 7.4 %all-to-all-done = bf16[32,2,4096]{2,1,0:T(2,128)(2,1)S(1)} async-done(((bf16[32,2,4096]{2,1,0:T(2,128)(2,1)}), bf16[32,2,4096]{2,1,0:T(2,128)(2,1)S(1)}, u32[]{:S(2)}, u32[]{:S(2)}) %all-to-all-start) | async-done | bytes 524320 | tf_op jit(solution)/shard_map/all_to_all | solution.py:24
  28.4 3.5 %all-to-all-start.2 = ((bf16[2,64,2048]{2,0,1:T(2,128)(2,1)}), bf16[2,64,2048]{2,0,1:T(2,128)(2,1)S(1)}, u32[]{:S(2)}, u32[]{:S(2)}) async-start(bf16[2,64,2048]{2,0,1:T(2,128)(2,1)} %copy.25), calls=%async_computation.2 | async-start | bytes 1048576 | tf_op jit(solution)/shard_map/all_to_all | solution.py:26
  31.9 0.2 reshape.34
  32.1 8.8 %fusion.10 = bf16[8,8,2048]{2,1,0:T(8,128)(2,1)S(1)} fusion(bf16[64,4096]{1,0:T(8,128)(2,1)S(1)} %reshape.34, bf16[1,4096,2048]{2,1,0:T(8,128)(2,1)} %param.6, f32[]{:T(128)} %bitcast.5), kind=kOutput, calls=%fused_computation.8 | convolution fusion | flops 1074003968 | bytes 17563652 | tf_op jit(solution)/shard_map/dot_general | solution.py:34
  40.9 1.2 %bitcast_multiply_fusion = bf16[32,8,2048]{2,1,0:T(8,128)(2,1)} fusion(bf16[32]{0:T(256)(128)(2,1)S(1)} %mul.42, bf16[8,8,2048]{2,1,0:T(8,128)(2,1)S(1)} %fusion.10), kind=kLoop, calls=%fused_computation.11 | loop fusion | flops 524288 | bytes 1310784 | tf_op jit(solution)/shard_map/mul | solution.py:38
  42.1 0.0 all-to-all-done.2
  42.1 3.6 %all-to-all-start.1 = ((bf16[32,8,2048]{2,1,0:T(8,128)(2,1)}), bf16[32,8,2048]{2,1,0:T(8,128)(2,1)}, u32[]{:S(2)}, u32[]{:S(2)}) async-start(bf16[32,8,2048]{2,1,0:T(8,128)(2,1)} %bitcast_multiply_fusion), calls=%async_computation.1 | async-start | bytes 2097152 | tf_op jit(solution)/shard_map/all_to_all | solution.py:40
  45.7 0.0 copy-done
  45.8 0.5 reshape.35
  46.3 0.2 copy.31
  46.5 1.1 %reshape.48 = bf16[8,2,8,32,64,1]{4,3,2,1,0,5:T(8,128)(2,1)S(1)} reshape(bf16[4,2,16,2048]{3,2,1,0:T(8,128)(2,1)S(1)} %bitcast.46) | data formatting | bytes 1048576 | tf_op jit(solution)/shard_map/reshape | solution.py:27
  47.5 1.3 %convolution_bitcast_fusion.1 = f32[8,2,8,32,64]{4,3,1,0,2:T(8,128)S(1)} fusion(bf16[8,2,8,32,64,1]{4,3,2,1,0,5:T(8,128)(2,1)S(1)} %reshape.48, bf16[8,64,8,64,1,1]{3,2,1,0,5,4:T(8,128)(2,1)S(1)} %bitcast.48), kind=kOutput, calls=%fused_computation.9 | convolution fusion | flops 268435456 | bytes 2097152 | tf_op jit(solution)/shard_map/pkqsd,bjqd->pkbsj/dot_general | solution.py:29
  48.8 0.2 copy.20
  49.0 0.7 reshape.37
  49.7 22.2 %all-to-all-done.1 = bf16[32,8,2048]{2,1,0:T(8,128)(2,1)} async-done(((bf16[32,8,2048]{2,1,0:T(8,128)(2,1)}), bf16[32,8,2048]{2,1,0:T(8,128)(2,1)}, u32[]{:S(2)}, u32[]{:S(2)}) %all-to-all-start.1) | async-done | bytes 1048608 | tf_op jit(solution)/shard_map/all_to_all | solution.py:40
  71.9 3.2 %fusion.3 = bf16[8,16,2048]{2,1,0:T(8,128)(2,1)} fusion(f32[8,16,2048]{2,1,0:T(8,128)S(1)} %reshape.37, bf16[32,8,2048]{2,1,0:T(8,128)(2,1)} %all-to-all-done.1, s32[32]{0:T(128)S(1)} %get-tuple-element.5, s32[16]{0:T(128)S(1)} %iota_add_fusion), kind=kOutput, calls=%fused_computation.5 | convolution fusion | flops 17302016 | bytes 2621632 | tf_op jit(solution)/shard_map/rpo,rt->pto/dot_general | solution.py:43
  (4 shorter events, 0.0 us)
Async XLA Ops:
  5.5 40.2 %copy-start = (bf16[512,512]{1,0:T(8,128)(2,1)S(1)}, bf16[512,512]{1,0:T(8,128)(2,1)}, u32[]{:S(2)}) copy-start(bf16[512,512]{1,0:T(8,128)(2,1)} %param.7) | copy-start | bytes 1572868
  5.5 22.9 %all-to-all-start = ((bf16[32,2,4096]{2,1,0:T(2,128)(2,1)}), bf16[32,2,4096]{2,1,0:T(2,128)(2,1)S(1)}, u32[]{:S(2)}, u32[]{:S(2)}) async-start(bf16[32,2,4096]{2,1,0:T(2,128)(2,1)} %copy.15), calls=%async_computation | async-start | bytes 1048576 | tf_op jit(solution)/shard_map/all_to_all | solution.py:24
  28.4 13.7 %all-to-all-start.2 = ((bf16[2,64,2048]{2,0,1:T(2,128)(2,1)}), bf16[2,64,2048]{2,0,1:T(2,128)(2,1)S(1)}, u32[]{:S(2)}, u32[]{:S(2)}) async-start(bf16[2,64,2048]{2,0,1:T(2,128)(2,1)} %copy.25), calls=%async_computation.2 | async-start | bytes 1048576 | tf_op jit(solution)/shard_map/all_to_all | solution.py:26
  42.1 29.8 %all-to-all-start.1 = ((bf16[32,8,2048]{2,1,0:T(8,128)(2,1)}), bf16[32,8,2048]{2,1,0:T(8,128)(2,1)}, u32[]{:S(2)}, u32[]{:S(2)}) async-start(bf16[32,8,2048]{2,1,0:T(8,128)(2,1)} %bitcast_multiply_fusion), calls=%async_computation.1 | async-start | bytes 2097152 | tf_op jit(solution)/shard_map/all_to_all | solution.py:40
where the time goes:
time: 75.8 us; the launch traced here: 75.2 us
  waiting for transfers between devices  29.6 us (39%)
  starting transfers between devices  14.4 us (19%)
  matrix products  13.3 us (18%)
  local copies, waits for them, and re-layouts  11.8 us (16%)
  between operations  3.27 us (4%)
  other arithmetic  2.74 us (4%)
    all_to_all x1, waiting for transfers between devices, per_device(): received = lax.all_to_all(outgoing, ('pair', 'virt'), 0, 0, tiled=True)  22.2 us
    dot_general x1, matrix products, per_device(): product = jnp.dot(chosen, integrals[0], preferred_element_type=jnp.float32)  8.79 us
    all_to_all x1, waiting for transfers between devices, per_device(): chosen = lax.all_to_all(picked, ('pair', 'virt'), 0, 0, tiled=True)  7.37 us
    all_to_all x1, starting transfers between devices, per_device(): chosen = lax.all_to_all(picked, ('pair', 'virt'), 0, 0, tiled=True)  7.33 us
    all_to_all x1, starting transfers between devices, per_device(): received = lax.all_to_all(outgoing, ('pair', 'virt'), 0, 0, tiled=True)  3.62 us
    all_to_all x1, starting transfers between devices, per_device(): lax.all_to_all(amps_pm[:, :, :out_cols], 'virt', split_axis=1, concat_axi...  3.47 us
    dot_general x1, matrix products, per_device(): jnp.einsum('rpo,rt->pto', received, one_hot, preferred_element_type=jnp.f...  3.24 us
    gather x1, local copies, waits for them, and re-layouts, per_device(): picked = jnp.take(amps_pm, tin_all, axis=1)  2.59 us
  transfers between devices with their start and end apart: 3, of which 2 were waited for; matrix products, arithmetic and copies ran while one was open for 25% of the time, Pallas kernels for 0%

commit v1 on v0

--- a/solution.py
+++ b/solution.py
@@ -6,6 +6,16 @@
 TILE = 64
 NVT = 8
 AS = 32
+
+
+def serve_the_wall(local_values):
+    kept_arr = jnp.concatenate(
+        lax.all_to_all(
+            jnp.stack(jnp.split(local_values, lax.axis_size("virt"), axis=1)), "virt", 0, 0
+        ),
+        0,
+    )
+    return kept_arr
 
 
 def per_device(amps_pm, integrals, fock_vv, blk_tiles, blk_mask):
@@ -23,7 +33,7 @@
     picked = jnp.transpose(picked, (1, 0, 2))
     chosen = lax.all_to_all(picked, ("pair", "virt"), 0, 0, tiled=True)
     chosen = chosen.reshape(n_dev * pm_rows, tile_len)
-    sub = lax.all_to_all(amps_pm[:, :, :out_cols], "virt", split_axis=1, concat_axis=0, tiled=True)
+    sub = serve_the_wall(amps_pm[:, :, :out_cols])
     sub = sub.reshape(p_grp, slab // NVT, NVT, AS, TILE)
     fock_four = fock_vv.reshape(NVT, TILE, NVT, TILE)
     onebody = jnp.einsum(

time: 75.8 us -> 74.5 us (0.983)
  waiting for transfers between devices: 29.6 us -> 24.3 us
  local copies, waits for them, and re-layouts: 11.8 us -> 13.7 us
  matrix products: 13.3 us -> 14.7 us
  other arithmetic: 2.74 us -> 3.56 us
    all_to_all x1, waiting for transfers between devices: 22.2 us -> 16.5 us  [per_device(): received = lax.all_to_all(outgoing, ('pair', 'virt'), 0, 0, tiled=True)]
    another operation x0 -> x2, local copies, waits for them, and re-layouts: none -> 3.19 us  [the longest x1 2.05 us: per_device(): sub = sub.reshape(p_grp, slab // NVT, NVT, AS, TILE)]
    dot_general x1, matrix products: 1.27 us -> 3.84 us  [per_device(): jnp.einsum('pkqsd,bjqd->pkbsj', sub, fock_four, preferred_element_type=jn...]
    reshape x1, local copies, waits for them, and re-layouts: 0.65 us -> 2.08 us  [per_device(): onebody = jnp.einsum('pkqsd,bjqd->pkbsj', sub, fock_four, preferred_eleme...]
    unnamed x3 -> x0, local copies, waits for them, and re-layouts: 1.34 us -> none
    dot_general x1, matrix products: 3.24 us -> 2.02 us  [per_device(): jnp.einsum('rpo,rt->pto', received, one_hot, preferred_element_type=jnp.f...]
    reshape x1, local copies, waits for them, and re-layouts: 0.53 us -> 1.65 us  [per_device(): fock_four = fock_vv.reshape(NVT, TILE, NVT, TILE)]
    slice x1 -> x0, local copies, waits for them, and re-layouts: 1.08 us -> none  [per_device(): amps_pm[:, :, :out_cols]]
  transfers between devices with their start and end apart: 3 -> 3, of which waited for: 2 -> 2; matrix products, arithmetic and copies ran while one was open for 25% -> 33% of each run, Pallas kernels for 0% -> 0%
where the time goes in v1:
time: 74.5 us; the launch traced here: 73.8 us
  waiting for transfers between devices  24.3 us (33%)
  matrix products  14.7 us (20%)
  starting transfers between devices  14.3 us (19%)
  local copies, waits for them, and re-layouts  13.7 us (18%)
  other arithmetic  3.56 us (5%)
  between operations  3.36 us (5%)
    all_to_all x1, waiting for transfers between devices, per_device(): received = lax.all_to_all(outgoing, ('pair', 'virt'), 0, 0, tiled=True)  16.5 us
    dot_general x1, matrix products, per_device(): product = jnp.dot(chosen, integrals[0], preferred_element_type=jnp.float32)  8.79 us
    all_to_all x1, waiting for transfers between devices, per_device(): chosen = lax.all_to_all(picked, ('pair', 'virt'), 0, 0, tiled=True)  7.72 us
    all_to_all x1, starting transfers between devices, per_device(): chosen = lax.all_to_all(picked, ('pair', 'virt'), 0, 0, tiled=True)  7.33 us
    dot_general x1, matrix products, per_device(): jnp.einsum('pkqsd,bjqd->pkbsj', sub, fock_four, preferred_element_type=jn...  3.84 us
    all_to_all x1, starting transfers between devices, per_device(): received = lax.all_to_all(outgoing, ('pair', 'virt'), 0, 0, tiled=True)  3.49 us
    all_to_all x1, starting transfers between devices, serve_the_wall(): lax.all_to_all(jnp.stack(jnp.split(local_values, lax.axis_size('virt'), a...  3.47 us
    gather x1, local copies, waits for them, and re-layouts, per_device(): picked = jnp.take(amps_pm, tin_all, axis=1)  2.59 us
  transfers between devices with their start and end apart: 3, of which 2 were waited for; matrix products, arithmetic and copies ran while one was open for 33% of the time, Pallas kernels for 0%

profile of v1, /device:TPU:0, one launch (start us, length us, event | category | flops | bytes accessed | tf_op | source)
XLA Modules:
  0.0 73.8 jit_solution(8951630119658892802)
XLA Ops:
  0.0 0.8 %slice_bitcast_fusion.4 = (s32[32]{0:T(128)S(1)}, s32[32]{0:T(128)S(1)}) fusion(s32[32,2]{0,1:T(2,128)} %param.8), kind=kLoop, calls=%fused_computation.29 | loop fusion | flops 96 | bytes 512 | tf_op jit(solution)/shard_map/eq | solution.py:52
  0.8 0.7 and_bitcast_fusion
  1.5 2.6 %gather_fusion = bf16[32,2,4096]{2,0,1:T(8,128)(2,1)S(1)} fusion(bf16[2,64,4096]{2,1,0:T(8,128)(2,1)} %param.5, s32[1024]{0:T(1024)S(1)} %pad_clamp_fusion), kind=kCustom, calls=%fused_computation | custom fusion | bytes 1048704 | tf_op jit(solution)/shard_map/jit(_take)/gather | solution.py:32
  4.0 0.1 broadcast_select_fusion
  4.2 1.3 %copy.11 = bf16[32,2,4096]{2,1,0:T(2,128)(2,1)} copy(bf16[32,2,4096]{2,0,1:T(8,128)(2,1)S(1)} %broadcast_select_fusion) | data formatting | bytes 1048576 | tf_op jit(solution)/shard_map/jit(_take)/select_n | solution.py:32
  5.5 7.3 %all-to-all-start = ((bf16[32,2,4096]{2,1,0:T(2,128)(2,1)}), bf16[32,2,4096]{2,1,0:T(2,128)(2,1)S(1)}, u32[]{:S(2)}, u32[]{:S(2)}) async-start(bf16[32,2,4096]{2,1,0:T(2,128)(2,1)} %copy.11), calls=%async_computation | async-start | bytes 1048576 | tf_op jit(solution)/shard_map/all_to_all | solution.py:34
  12.8 0.8 %constant_dynamic-slice_fusion = s32[1,2]{0,1:T(2,128)S(1)} fusion(s32[32,2]{0,1:T(2,128)} %param.8, s32[]{:T(128)S(6)} %select_n.29), kind=kLoop, calls=%fused_computation.30 | loop fusion | bytes 20 | tf_op jit(solution)/shard_map/jit(dynamic_index_in_dim)/dynamic_slice | solution.py:42
  13.6 0.5 slice.17
  16.7 0.1 mul.42
  16.8 1.2 %dynamic_slice.8 = s32[1]{0:T(128)} dynamic-slice(s32[32]{0:T(128)} %param.9, s32[]{:T(128)S(6)} %select_n.29), dynamic_slice_sizes={1} | dynamic-slice | bytes 12 | tf_op jit(solution)/shard_map/jit(dynamic_index_in_dim)/dynamic_slice | solution.py:43
  18.7 1.1 %slice_bitcast_fusion.3 = (bf16[1,2,16,2048]{3,2,1,0:T(8,128)(2,1)S(1)}, bf16[1,2,16,2048]{3,2,1,0:T(8,128)(2,1)S(1)}, bf16[1,2,16,2048]{3,2,1,0:T(8,128)(2,1)S(1)}, bf16[1,2,16,2048]{3,2,1,0:T(8,128)(2,1)S(1)}) fusion(bf16[2,64,4096]{2,1,0:T(8,128)(2,1)} %param.5), kind=kLoop, calls=%fused_computation.19 | loop fusion | bytes 1048576 | tf_op jit(solution)/shard_map/stack | solution.py:14
  19.9 0.9 %pad_maximum_fusion = bf16[4,2,16,2048]{3,2,1,0:T(8,128)(2,1)} fusion(bf16[1,2,16,2048]{3,2,1,0:T(8,128)(2,1)S(1)} %get-tuple-element.7, bf16[1,2,16,2048]{3,2,1,0:T(8,128)(2,1)S(1)} %get-tuple-element.8, bf16[1,2,16,2048]{3,2,1,0:T(8,128)(2,1)S(1)} %get-tuple-element.6, bf16[1,2,16,2048]{3,2,1,0:T(8,128)(2,1)S(1)} %get-tuple-element.5), kind=kLoop, calls=%fused_computation.14 | loop fusion | flops 786432 | bytes 1048576 | tf_op jit(solution)/shard_map/stack | solution.py:14
  20.7 7.7 %all-to-all-done = bf16[32,2,4096]{2,1,0:T(2,128)(2,1)S(1)} async-done(((bf16[32,2,4096]{2,1,0:T(2,128)(2,1)}), bf16[32,2,4096]{2,1,0:T(2,128)(2,1)S(1)}, u32[]{:S(2)}, u32[]{:S(2)}) %all-to-all-start) | async-done | bytes 524320 | tf_op jit(solution)/shard_map/all_to_all | solution.py:34
  28.4 3.5 %all-to-all-start.2 = ((bf16[4,2,16,2048]{3,2,1,0:T(8,128)(2,1)}), bf16[4,2,16,2048]{3,2,1,0:T(8,128)(2,1)S(1)}, u32[]{:S(2)}, u32[]{:S(2)}) async-start(bf16[4,2,16,2048]{3,2,1,0:T(8,128)(2,1)} %pad_maximum_fusion), calls=%async_computation.2 | async-start | bytes 1048576 | tf_op jit(solution)/shard_map/all_to_all | solution.py:13
  31.9 0.2 reshape.30
  32.1 8.8 %fusion.10 = bf16[8,8,2048]{2,1,0:T(8,128)(2,1)S(1)} fusion(bf16[64,4096]{1,0:T(8,128)(2,1)S(1)} %reshape.30, bf16[1,4096,2048]{2,1,0:T(8,128)(2,1)} %param.6, f32[]{:T(128)} %bitcast.5), kind=kOutput, calls=%fused_computation.8 | convolution fusion | flops 1074003968 | bytes 17563652 | tf_op jit(solution)/shard_map/dot_general | solution.py:44
  40.9 1.1 %bitcast_multiply_fusion = bf16[32,8,2048]{2,1,0:T(8,128)(2,1)} fusion(bf16[32]{0:T(256)(128)(2,1)S(1)} %mul.42, bf16[8,8,2048]{2,1,0:T(8,128)(2,1)S(1)} %fusion.10), kind=kLoop, calls=%fused_computation.12 | loop fusion | flops 524288 | bytes 1310784 | tf_op jit(solution)/shard_map/mul | solution.py:48
  42.1 0.0 all-to-all-done.2
  42.1 3.5 %all-to-all-start.1 = ((bf16[32,8,2048]{2,1,0:T(8,128)(2,1)}), bf16[32,8,2048]{2,1,0:T(8,128)(2,1)S(1)}, u32[]{:S(2)}, u32[]{:S(2)}) async-start(bf16[32,8,2048]{2,1,0:T(8,128)(2,1)} %bitcast_multiply_fusion), calls=%async_computation.1 | async-start | bytes 2097152 | tf_op jit(solution)/shard_map/all_to_all | solution.py:50
  45.6 1.6 %reshape.31 = bf16[8,64,8,64]{3,2,1,0:T(8,128)(2,1)S(1)} reshape(bf16[512,512]{1,0:T(8,128)(2,1)} %param.7) | data formatting | bytes 1048576 | tf_op jit(solution)/shard_map/reshape | solution.py:38
  47.2 2.1 %reshape.42 = bf16[8,2,8,32,64,1]{4,3,2,1,0,5:T(8,128)(2,1)} reshape(bf16[4,2,16,2048]{3,2,1,0:T(8,128)(2,1)S(1)} %all-to-all-done.2) | data formatting | bytes 1048576 | tf_op jit(solution)/shard_map/reshape;reshape | solution.py:37
  49.3 3.8 %convolution_bitcast_fusion.1 = f32[8,2,8,32,64]{4,3,2,1,0:T(8,128)} fusion(bf16[8,64,8,64,1,1]{3,2,1,0,5,4:T(8,128)(2,1)S(1)} %bitcast.52, bf16[8,2,8,32,64,1]{4,3,2,1,0,5:T(8,128)(2,1)} %reshape.42), kind=kOutput, calls=%fused_computation.9 | convolution fusion | flops 268435456 | bytes 2097152 | tf_op jit(solution)/shard_map/pkqsd,bjqd->pkbsj/dot_general | solution.py:39
  53.1 2.1 %reshape.32 = f32[8,16,2048]{2,1,0:T(8,128)S(1)} reshape(f32[8,2,8,32,64]{4,3,2,1,0:T(8,128)} %convolution_bitcast_fusion.1) | data formatting | bytes 2097152 | tf_op jit(solution)/shard_map/reshape | solution.py:41
  55.2 16.5 %all-to-all-done.1 = bf16[32,8,2048]{2,1,0:T(8,128)(2,1)S(1)} async-done(((bf16[32,8,2048]{2,1,0:T(8,128)(2,1)}), bf16[32,8,2048]{2,1,0:T(8,128)(2,1)S(1)}, u32[]{:S(2)}, u32[]{:S(2)}) %all-to-all-start.1) | async-done | bytes 1048608 | tf_op jit(solution)/shard_map/all_to_all | solution.py:50
  71.8 2.0 %fusion.3 = bf16[8,16,2048]{2,1,0:T(8,128)(2,1)} fusion(f32[8,16,2048]{2,1,0:T(8,128)S(1)} %reshape.32, bf16[32,8,2048]{2,1,0:T(8,128)(2,1)S(1)} %all-to-all-done.1, s32[32]{0:T(128)S(1)} %get-tuple-element.9, s32[16]{0:T(128)S(1)} %iota_add_fusion), kind=kOutput, calls=%fused_computation.5 | convolution fusion | flops 17302016 | bytes 2621632 | tf_op jit(solution)/shard_map/rpo,rt->pto/dot_general | solution.py:53
  (4 shorter events, 0.0 us)
Async XLA Ops:
  5.5 22.9 %all-to-all-start = ((bf16[32,2,4096]{2,1,0:T(2,128)(2,1)}), bf16[32,2,4096]{2,1,0:T(2,128)(2,1)S(1)}, u32[]{:S(2)}, u32[]{:S(2)}) async-start(bf16[32,2,4096]{2,1,0:T(2,128)(2,1)} %copy.11), calls=%async_computation | async-start | bytes 1048576 | tf_op jit(solution)/shard_map/all_to_all | solution.py:34
  28.4 13.6 %all-to-all-start.2 = ((bf16[4,2,16,2048]{3,2,1,0:T(8,128)(2,1)}), bf16[4,2,16,2048]{3,2,1,0:T(8,128)(2,1)S(1)}, u32[]{:S(2)}, u32[]{:S(2)}) async-start(bf16[4,2,16,2048]{3,2,1,0:T(8,128)(2,1)} %pad_maximum_fusion), calls=%async_computation.2 | async-start | bytes 1048576 | tf_op jit(solution)/shard_map/all_to_all | solution.py:13
  42.1 29.7 %all-to-all-start.1 = ((bf16[32,8,2048]{2,1,0:T(8,128)(2,1)}), bf16[32,8,2048]{2,1,0:T(8,128)(2,1)S(1)}, u32[]{:S(2)}, u32[]{:S(2)}) async-start(bf16[32,8,2048]{2,1,0:T(8,128)(2,1)} %bitcast_multiply_fusion), calls=%async_computation.1 | async-start | bytes 2097152 | tf_op jit(solution)/shard_map/all_to_all | solution.py:50
